TPU v7x, 128 devices: a whole 4x4x4 slice. The times are simulated.
128 devices in a mesh: row: 8 (over x, core), col: 16 (over y, z).
Axes of the slice: x: 4, y: 4, z: 4, core: 2. Of those that a mesh axis runs over, the one named last changes fastest.
Arguments:
- front_matrix: float32 [16384, 16384], P('row', 'col'), may hold values from -2.5 to 202.5, as said below
- child_schur: float32 [2, 8192, 8192], P(None, 'row', 'col'), may hold values from -1.25 to 1.25
- child_index: int32 [2, 128], replicated, may hold values from 0 to 255, as said below
- child_valid: int32 [2, 128], replicated, may hold values 0 or 1
Outputs:
- trailing: float32 [16384, 16384], P('row', 'col')
- panel_factor: float32 [16384, 512], P('row')
Inputs may be any that keep to these rules, and one draw needn't show every extreme that they name: `front_matrix`: off the logical diagonal the entries lie in -2.5 to 2.5, on it in 97.5 to 202.5. `child_index`: each child's 128 entries are distinct front blocks. Among the child blocks a that share a mod 8, exactly 2 land in front blocks of each value mod 8; among the child blocks b that share b mod 16, at most 1 land in front blocks of any one value mod 16, and some value takes exactly 1.
All inputs are finite; a program needn't handle non-finite values.
Results may differ from a plain program's by a relative error of at most 0.00005.
Values sent between devices are 32-bit elements; how exact they have to be, the bound alone decides.
No kernel may reach another device: no remote copies, remote signals or barrier semaphores. Data moves between devices by JAX's collectives and lax.ppermute only.
A program may use at most 256 MiB of HBM per device.

v0:
```python
import jax
import jax.numpy as jnp
from jax import lax
from jax.sharding import PartitionSpec as P

CHILD = 8192
PANEL = 512
BLK = 64
exact_mode = lax.Precision.HIGHEST


def take_slabs(source, indices):
    return jnp.take(source, indices, axis=0)


def on_device(front_matrix, child_schur, child_index, child_valid):
    row_count = lax.axis_size("row")
    col_count = lax.axis_size("col")
    row_place = lax.axis_index("row")
    col_place = lax.axis_index("col")
    local_rows, local_cols = front_matrix.shape
    row_blocks = local_rows // BLK
    col_blocks = local_cols // BLK
    child_blocks = CHILD // BLK
    child_rowblk = child_schur.shape[1] // BLK
    child_colblk = child_schur.shape[2] // BLK
    per_owner = child_blocks // (row_count * row_count)
    col_multi = max(1, child_blocks // (col_count * col_count))
    row_slots = row_count * per_owner
    col_slots = col_count * col_multi
    validity = child_valid.astype(jnp.float32)
    all_blocks = jnp.arange(child_blocks)
    owner_row = child_index % row_count
    owner_col = child_index % col_count
    sender_row = all_blocks % row_count
    sender_col = all_blocks % col_count
    before = all_blocks[None, :] < all_blocks[:, None]
    earlier_row = (sender_row[:, None] == sender_row[None, :]) & before
    earlier_col = (sender_col[:, None] == sender_col[None, :]) & before
    row_rank = jnp.sum(
        (earlier_row[None] & (owner_row[:, :, None] == owner_row[:, None, :])).astype(jnp.int32),
        axis=2,
    )
    col_rank = jnp.sum(
        (earlier_col[None] & (owner_col[:, :, None] == owner_col[:, None, :])).astype(jnp.int32),
        axis=2,
    )
    row_key = owner_row * per_owner + row_rank
    col_key = owner_col * col_multi + col_rank
    local_arow = row_place + row_count * jnp.arange(child_rowblk)
    mine_rowkey = jnp.take(row_key, local_arow, axis=1)
    row_hit_send = mine_rowkey[:, :, None] == jnp.arange(row_slots)[None, None, :]
    src_row = jnp.sum(
        row_hit_send.astype(jnp.int32) * jnp.arange(child_rowblk)[None, :, None], axis=1
    )
    local_bcol = col_place + col_count * jnp.arange(child_colblk)
    mine_colkey = jnp.take(col_key, local_bcol, axis=1)
    col_hit_send = mine_colkey[:, :, None] == jnp.arange(col_slots)[None, None, :]
    src_col = jnp.sum(
        col_hit_send.astype(jnp.int32) * jnp.arange(child_colblk)[None, :, None], axis=1
    )
    has_col = jnp.sum(col_hit_send.astype(jnp.float32), axis=1)
    blocks = child_schur.reshape(2, child_rowblk, BLK, child_colblk * BLK)
    outgoing = jax.vmap(take_slabs)(blocks, src_row)
    outgoing = outgoing.reshape(2, row_slots * BLK, child_colblk * BLK)
    section_one = lax.all_to_all(outgoing, "row", split_axis=1, concat_axis=1, tiled=True)
    flipped = jnp.swapaxes(section_one, 1, 2).reshape(2, child_colblk, BLK, row_slots * BLK)
    onward = jax.vmap(take_slabs)(flipped, src_col) * has_col[:, :, None, None]
    onward = onward.reshape(2, col_slots * BLK, row_slots * BLK)
    section_two = lax.all_to_all(onward, "col", split_axis=1, concat_axis=1, tiled=True)
    arrived = section_two.reshape(2, col_slots, BLK, row_slots * BLK)
    front_rowblk = row_place + row_count * jnp.arange(row_blocks)
    match_rows = (child_index[:, None, :] == front_rowblk[None, :, None]).astype(jnp.int32)
    row_slot_of = sender_row[None, :] * per_owner + row_rank
    row_source = jnp.sum(match_rows * row_slot_of[:, None, :], axis=2)
    row_weight = jnp.sum(match_rows.astype(jnp.float32) * validity[:, None, :], axis=2)
    front_colblk = col_place + col_count * jnp.arange(col_blocks)
    match_cols = (child_index[:, None, :] == front_colblk[None, :, None]).astype(jnp.int32)
    col_slot_of = sender_col[None, :] * col_multi + col_rank
    col_source = jnp.sum(match_cols * col_slot_of[:, None, :], axis=2)
    col_weight = jnp.sum(match_cols.astype(jnp.float32) * validity[:, None, :], axis=2)
    by_col = jax.vmap(take_slabs)(arrived, col_source) * col_weight[:, :, None, None]
    by_col = by_col.reshape(2, local_cols, row_slots * BLK)
    unflipped = jnp.swapaxes(by_col, 1, 2).reshape(2, row_slots, BLK, local_cols)
    placed = jax.vmap(take_slabs)(unflipped, row_source) * row_weight[:, :, None, None]
    placed = placed.reshape(2, local_rows, local_cols)
    extended = front_matrix + placed[0] + placed[1]
    panel_width = PANEL // BLK
    spread = col_count // panel_width
    lead = extended[:, :BLK]
    lifted = lax.ppermute(
        lead,
        "col",
        [(c, c + panel_width * s) for s in range(1, spread) for c in range(panel_width)],
    )
    mine = jnp.where(col_place < panel_width, lead, lifted)
    part_rows = local_rows // spread
    part = lax.dynamic_slice_in_dim(mine, col_place // panel_width * part_rows, part_rows, axis=0)
    gathered = lax.all_gather(part, "col", axis=0, tiled=False)
    gathered = gathered.reshape(spread, panel_width, part_rows, BLK)
    panel_cols = gathered.transpose(0, 2, 1, 3).reshape(local_rows, PANEL)
    corner = lax.all_gather(panel_cols[: PANEL // row_count], "row", axis=0, tiled=True)
    lower_factor = jnp.linalg.cholesky(corner)
    solved = jax.scipy.linalg.solve_triangular(lower_factor, panel_cols.T, lower=True).T
    logical_blk = jnp.arange(row_blocks) * row_count + row_place
    factor_blocks = lower_factor.reshape(panel_width, BLK, PANEL)
    picked = jnp.take(factor_blocks, jnp.minimum(logical_blk, panel_width - 1), axis=0)
    in_panel = (logical_blk < panel_width)[:, None, None]
    panel_factor = jnp.where(in_panel, picked, solved.reshape(row_blocks, BLK, PANEL)).reshape(
        local_rows, PANEL
    )
    ratio = col_count // row_count
    arranged = panel_factor.reshape(col_blocks, ratio, BLK, PANEL)
    chosen = lax.dynamic_index_in_dim(arranged, col_place // row_count, axis=1, keepdims=False)
    chosen = chosen.reshape(col_blocks * BLK, PANEL)
    pairs = []
    for r0 in range(row_count):
        for c1 in range(col_count):
            dest_row = c1 % row_count
            dest_col = r0 + row_count * (c1 // row_count)
            pairs.append((r0 * col_count + c1, dest_row * col_count + dest_col))
    across = lax.ppermute(chosen, ("row", "col"), pairs)
    update = jnp.einsum("rp,cp->rc", panel_factor, across, precision=exact_mode)
    logical_row = jnp.arange(local_rows) // BLK * row_count + row_place
    logical_col = jnp.arange(local_cols) // BLK * col_count + col_place
    retained = (logical_row >= panel_width)[:, None] & (logical_col >= panel_width)[None, :]
    trailing = jnp.where(retained, extended - update, jnp.zeros_like(update))
    return (trailing, panel_factor)


def solution(mesh):
    in_specs = (P("row", "col"), P(None, "row", "col"), P(), P())
    out_specs = (P("row", "col"), P("row", None))
    return jax.shard_map(
        on_device, mesh=mesh, in_specs=in_specs, out_specs=out_specs, check_vma=False
    )
```

profile of v0, /device:TPU:7, one launch (start us, length us, event | category | flops | bytes accessed | tf_op | source)
XLA Modules:
  0.0 768.0 jit_solution(1678104543497816341)
XLA Ops:
  29.0 46.6 %all-to-all-done = f32[2,1024,512]{2,0,1:T(2,128)} async-done(((f32[2,1024,512]{2,0,1:T(2,128)}), f32[2,1024,512]{2,0,1:T(2,128)}, u32[]{:S(2)}, u32[]{:S(2)}) %all-to-all-start) | async-done | bytes 4194336 | tf_op jit(solution)/shard_map/all_to_all | solution.py:66
  75.6 7.2 copy.127
  82.8 6.7 gather_fusion.4
  93.4 12.9 %copy.128 = f32[2,1024,1024]{2,0,1:T(2,128)} copy(f32[2,1024,1024]{2,1,0:T(8,128)S(1)} %fusion.2) | data formatting | bytes 16777216 | tf_op jit(solution)/shard_map/mul | solution.py:68
  106.3 8.1 %all-to-all-start.1 = ((f32[2,1024,1024]{2,0,1:T(2,128)}), f32[2,1024,1024]{2,0,1:T(2,128)}, u32[]{:S(2)}, u32[]{:S(2)}) async-start(f32[2,1024,1024]{2,0,1:T(2,128)} %copy.128), calls=%async_computation.1 | async-start | bytes 16777216 | tf_op jit(solution)/shard_map/all_to_all | solution.py:70
  115.9 140.9 %all-to-all-done.1 = f32[2,1024,1024]{2,0,1:T(2,128)} async-done(((f32[2,1024,1024]{2,0,1:T(2,128)}), f32[2,1024,1024]{2,0,1:T(2,128)}, u32[]{:S(2)}, u32[]{:S(2)}) %all-to-all-start.1) | async-done | bytes 8388640 | tf_op jit(solution)/shard_map/all_to_all | solution.py:70
  256.8 9.5 %copy.129 = f32[2,1024,1024]{2,1,0:T(8,128)} copy(f32[2,1024,1024]{2,0,1:T(2,128)} %all-to-all-done.1) | data formatting | bytes 16777216 | tf_op jit(solution)/shard_map/all_to_all | solution.py:70
  266.3 7.7 %gather_fusion.5 = f32[32,64,1024]{2,1,0:T(8,128)} fusion(f32[2,16,64,1024]{3,2,1,0:T(8,128)} %bitcast.129, s32[32]{0:T(128)S(1)} %reshape.535), kind=kCustom, calls=%fused_computation.5 | custom fusion | bytes 16777472 | tf_op jit(solution)/shard_map/vmap(jit(_take))/gather | solution.py:13
  274.0 6.0 fusion.1
  280.0 8.7 %copy.130 = f32[2,1024,1024]{2,1,0:T(8,128)} copy(f32[2,1024,1024]{1,2,0:T(8,128)} %fusion.1) | data formatting | bytes 16777216 | tf_op jit(solution)/shard_map/transpose | solution.py:84
  288.7 12.5 %gather_fusion.6 = f32[64,64,1024]{2,1,0:T(8,128)} fusion(f32[2,16,64,1024]{3,2,1,0:T(8,128)} %bitcast.124, s32[64]{0:T(128)S(1)} %reshape.541), kind=kCustom, calls=%fused_computation.6 | custom fusion | bytes 33554944 | tf_op jit(solution)/shard_map/vmap(jit(_take))/gather | solution.py:13
  301.2 7.3 select_multiply_fusion
  308.5 6.7 fusion.77
  315.2 9.7 %bitcast_add_fusion = f32[2048,1024]{1,0:T(8,128)S(1)} fusion(f32[1,32,64,1024]{3,2,1,0:T(8,128)} %get-tuple-element.35, f32[2048,1024]{1,0:T(8,128)} %param.4, f32[1,32,64,1024]{3,2,1,0:T(8,128)} %get-tuple-element.34), kind=kLoop, calls=%fused_computation.10 | loop fusion | flops 4194304 | bytes 33554432 | tf_op jit(solution)/shard_map/add | solution.py:87
  330.2 8.5 %collective-permute-done = f32[2048,64]{0,1:T(8,128)S(1)} collective-permute-done((f32[2048,64]{0,1:T(8,128)S(1)}, f32[2048,64]{0,1:T(8,128)S(1)}, u32[]{:S(2)}, u32[]{:S(2)}) %collective-permute-start) | collective-permute-done | bytes 524320 | tf_op jit(solution)/shard_map/ppermute | solution.py:91
  339.9 84.5 %all-gather.6.cloned.1.call-done = f32[16384,64]{1,0:T(8,128)} async-done(((f32[1024,64]{1,0:T(8,128)}), f32[16384,64]{1,0:T(8,128)}) %all-gather.6.cloned.1.call-update) | async-done | bytes 4194320 | tf_op jit(solution)/shard_map/all_gather | solution.py:99
  424.4 9.0 %copy.133 = f32[2,8,1024,64]{2,0,3,1:T(2,128)} copy(f32[2,8,1024,64]{3,2,1,0:T(8,128)} %bitcast.141) | data formatting | bytes 8388608 | tf_op jit(solution)/shard_map/reshape | solution.py:100
  440.8 21.5 %all-gather.4.cloned.1.call-done = f32[512,512]{1,0:T(8,128)} async-done(((f32[64,512]{1,0:T(8,128)}), f32[512,512]{1,0:T(8,128)}) %all-gather.4.cloned.1.call-update) | async-done | bytes 1048592 | tf_op jit(solution)/shard_map/all_gather | solution.py:102
  465.3 11.7 %cholesky.104 = f32[128,128]{1,0:T(8,128)S(1)} custom-call(f32[128,128]{1,0:T(8,128)S(1)} %cholesky.266), custom_call_target="Cholesky" | custom-call | tf_op jit(solution)/shard_map/jit(cholesky)/cholesky | solution.py:103
  477.2 9.8 %custom-call.31 = f32[1,128,128]{1,2,0:T(8,128)S(1)} custom-call(f32[1,128,128]{2,1,0:T(8,128)S(1)} %get-tuple-element.45), custom_call_target="InvertDiagBlocksLowerTriangular" | custom-call | tf_op jit(solution)/shard_map/jit(cholesky)/cholesky | solution.py:103
  487.7 11.9 %cholesky.217 = f32[128,128]{1,0:T(8,128)S(1)} custom-call(f32[128,128]{1,0:T(8,128)S(1)} %cholesky.270), custom_call_target="Cholesky" | custom-call | tf_op jit(solution)/shard_map/jit(cholesky)/cholesky | solution.py:103
  500.9 9.8 %custom-call.32 = f32[1,128,128]{1,2,0:T(8,128)S(1)} custom-call(f32[1,128,128]{2,1,0:T(8,128)S(1)} %get-tuple-element.42), custom_call_target="InvertDiagBlocksLowerTriangular" | custom-call | tf_op jit(solution)/shard_map/jit(cholesky)/cholesky | solution.py:103
  511.4 11.7 %cholesky.238 = f32[128,128]{1,0:T(8,128)S(1)} custom-call(f32[128,128]{1,0:T(8,128)S(1)} %cholesky.275), custom_call_target="Cholesky" | custom-call | tf_op jit(solution)/shard_map/jit(cholesky)/cholesky | solution.py:103
  523.8 9.8 %custom-call.33 = f32[1,128,128]{1,2,0:T(8,128)S(1)} custom-call(f32[1,128,128]{2,1,0:T(8,128)S(1)} %get-tuple-element.39), custom_call_target="InvertDiagBlocksLowerTriangular" | custom-call | tf_op jit(solution)/shard_map/jit(cholesky)/cholesky | solution.py:103
  534.2 11.9 %cholesky.255 = f32[128,128]{1,0:T(8,128)S(1)} custom-call(f32[128,128]{1,0:T(8,128)S(1)} %convolution_subtract_fusion.4), custom_call_target="Cholesky" | custom-call | tf_op jit(solution)/shard_map/jit(cholesky)/cholesky | solution.py:103
  549.7 10.5 %while.1 = (s32[]{:T(128)}, f32[512,512]{1,0:T(8,128)S(1)}, s32[4,2]{0,1:T(2,128)S(1)}, f32[4,128,128]{2,1,0:T(8,128)}, s32[]{:T(128)}) while((s32[]{:T(128)}, f32[512,512]{1,0:T(8,128)S(1)}, s32[4,2]{0,1:T(2,128)S(1)}, f32[4,128,128]{2,1,0:T(8,128)}, s32[]{:T(128)}) %tuple.44), condition=%wide.while_cond, body=%wide.while_body.sunk | while | flops 2 | bytes 132705 | solution.py:104
  560.2 40.2 %custom-call.34 = f32[4,128,128]{1,2,0:T(8,128)S(1)} custom-call(f32[4,128,128]{2,1,0:T(8,128)} %get-tuple-element.9), custom_call_target="InvertDiagBlocksLowerTriangular" | custom-call | tf_op jit(solution)/shard_map/jit(_solve_triangular)/triangular_solve | solution.py:104
  629.5 7.2 collective-permute-start.1
  637.1 5.7 copy.136
  642.8 5.4 select_select_fusion
  653.5 75.5 %collective-permute-done.1 = f32[1024,512]{1,0:T(8,128)} collective-permute-done((f32[1024,512]{1,0:T(8,128)}, f32[1024,512]{1,0:T(8,128)}, u32[]{:S(2)}, u32[]{:S(2)}) %collective-permute-start.1) | collective-permute-done | bytes 2097184 | tf_op jit(solution)/shard_map/ppermute | solution.py:122
  729.1 31.7 %subtract_select_fusion = f32[2048,1024]{1,0:T(8,128)} fusion(f32[2048,1024]{1,0:T(8,128)} %copy-done, pred[1024]{0:T(1024)(128)(4,1)S(1)} %fusion.54, pred[2048]{0:T(1024)(128)(4,1)S(1)} %fusion.48, f32[2048,512]{0,1:T(8,128)} %select_select_fusion, f32[1024,512]{1,0:T(8,128)} %collective-permute-done.1), kind=kOutput, calls=%fused_computation.17 | convolution fusion | flops 12891193344 | bytes 23071744 | tf_op jit(solution)/shard_map/rp,cp->rc/dot_general | solution.py:123
  (153 shorter events, 94.1 us)
Async XLA Ops:
  23.4 52.2 %all-to-all-start = ((f32[2,1024,512]{2,0,1:T(2,128)}), f32[2,1024,512]{2,0,1:T(2,128)}, u32[]{:S(2)}, u32[]{:S(2)}) async-start(f32[2,1024,512]{2,0,1:T(2,128)} %copy.126), calls=%async_computation | async-start | bytes 8388608 | tf_op jit(solution)/shard_map/all_to_all | solution.py:66
  106.3 8.3 %copy-start.7 = (s32[2,128]{1,0:T(2,128)S(1)}, s32[2,128]{1,0:T(2,128)}, u32[]{:S(2)}) copy-start(s32[2,128]{1,0:T(2,128)} %param.6) | copy-start | bytes 3076
  106.3 8.8 %copy-start.8 = (s32[2,128]{1,0:T(2,128)S(1)}, s32[2,128]{1,0:T(2,128)}, u32[]{:S(2)}) copy-start(s32[2,128]{1,0:T(2,128)} %param.7) | copy-start | bytes 3076
  106.3 150.5 %all-to-all-start.1 = ((f32[2,1024,1024]{2,0,1:T(2,128)}), f32[2,1024,1024]{2,0,1:T(2,128)}, u32[]{:S(2)}, u32[]{:S(2)}) async-start(f32[2,1024,1024]{2,0,1:T(2,128)} %copy.128), calls=%async_computation.1 | async-start | bytes 16777216 | tf_op jit(solution)/shard_map/all_to_all | solution.py:70
  114.4 310.0 %all-gather.6.cloned.1.call-start = ((), (), s32[]{:S(2)}) async-start(), calls=%async_computation.3 | async-start | bytes 8912896 | tf_op jit(solution)/shard_map/all_gather | solution.py:99
  325.0 3.4 copy-start
  328.8 9.9 %collective-permute-start = (f32[2048,64]{0,1:T(8,128)S(1)}, f32[2048,64]{0,1:T(8,128)S(1)}, u32[]{:S(2)}, u32[]{:S(2)}) collective-permute-start(f32[2048,64]{0,1:T(8,128)S(1)} %copy.131), channel_id=1, source_target_pairs={{0,8},{1,9},{2,10},{3,11},{4,12},{5,13},{6,14},{7,15},{16,24},{17,... | collective-permute-start | bytes 1572872 | tf_op jit(solution)/shard_map/ppermute | solution.py:91
  339.8 122.5 %all-gather.4.cloned.1.call-start = ((), (), s32[]{:S(2)}) async-start(), calls=%async_computation.2 | async-start | bytes 1179648 | tf_op jit(solution)/shard_map/all_gather | solution.py:102
  437.6 2.0 copy-start.1
  560.2 42.6 %copy-start.6 = (f32[512,512]{1,0:T(8,128)}, f32[512,512]{1,0:T(8,128)S(1)}, u32[]{:S(2)}) copy-start(f32[512,512]{1,0:T(8,128)S(1)} %get-tuple-element.112) | copy-start | bytes 3145732
  600.4 5.7 copy-start.2
  609.4 4.2 copy-start.3
  613.7 1.1 copy-start.5
  629.5 99.5 %collective-permute-start.1 = (f32[1024,512]{1,0:T(8,128)}, f32[1024,512]{1,0:T(8,128)}, u32[]{:S(2)}, u32[]{:S(2)}) collective-permute-start(f32[1024,512]{1,0:T(8,128)} %bitcast.40), channel_id=1, source_target_pairs={{0,0},{1,16},{2,32},{3,48},{4,64},{5,80},{6,96},{7,112},{8,8},{9,2... | collective-permute-start | bytes 6291464 | tf_op jit(solution)/shard_map/ppermute | solution.py:122
  637.1 5.7 copy-start.4
Sparse Core Ops, SparseCore 0:
  339.9 84.4 all-gather.5
  440.5 21.7 all-gather.3
where the time goes:
time: 777 us; the launch traced here: 768 us
  waiting for transfers between devices  378 us (49%)
  other arithmetic  166 us (21%)
  local copies, waits for them, and re-layouts  138 us (18%)
  matrix products  46.7 us (6%)
  starting transfers between devices  22 us (3%)
  between operations  17.6 us (2%)
    all_to_all x1, waiting for transfers between devices, on_device(): lax.all_to_all(onward, 'col', split_axis=1, concat_axis=1, tiled=True)  141 us
    all_gather x1, waiting for transfers between devices, on_device(): gathered = lax.all_gather(part, 'col', axis=0, tiled=False)  84.5 us
    another operation x15, other arithmetic, on_device(): lower_factor = jnp.linalg.cholesky(corner)  79.5 us
    ppermute x1, waiting for transfers between devices, on_device(): across = lax.ppermute(chosen, ('row', 'col'), pairs)  75.5 us
    all_to_all x1, waiting for transfers between devices, on_device(): lax.all_to_all(outgoing, 'row', split_axis=1, concat_axis=1, tiled=True)  46.6 us
    another operation x3, other arithmetic, on_device(): jax.scipy.linalg.solve_triangular(lower_factor, panel_cols.T, lower=True)  40.4 us
    gather x8, local copies, waits for them, and re-layouts, take_slabs(): return jnp.take(source, indices, axis=0)  32.2 us
    dot_general x1, matrix products, on_device(): update = jnp.einsum('rp,cp->rc', panel_factor, across, precision=exact_mode)  31.7 us
  transfers between devices with their start and end apart: 6, of which 6 were waited for; matrix products, arithmetic and copies ran while one was open for 2% of the time, Pallas kernels for 0%

commit v1 on v0

--- a/solution.py
+++ b/solution.py
@@ -99,7 +99,12 @@
     gathered = lax.all_gather(part, "col", axis=0, tiled=False)
     gathered = gathered.reshape(spread, panel_width, part_rows, BLK)
     panel_cols = gathered.transpose(0, 2, 1, 3).reshape(local_rows, PANEL)
-    corner = lax.all_gather(panel_cols[: PANEL // row_count], "row", axis=0, tiled=True)
+    corner = jnp.concatenate(
+        lax.all_to_all(
+            jnp.stack([panel_cols[: PANEL // row_count]] * lax.axis_size("row")), "row", 0, 0
+        ),
+        axis=0,
+    )
     lower_factor = jnp.linalg.cholesky(corner)
     solved = jax.scipy.linalg.solve_triangular(lower_factor, panel_cols.T, lower=True).T
     logical_blk = jnp.arange(row_blocks) * row_count + row_place

time: 777 us -> 771 us (level)
  waiting for transfers between devices: 378 us -> 369 us
    all_gather x1 -> x0, waiting for transfers between devices: 21.5 us -> none  [on_device(): lax.all_gather(panel_cols[:PANEL // row_count], 'row', axis=0, tiled=True)]
    all_to_all x0 -> x1, waiting for transfers between devices: none -> 12.4 us  [on_device(): lax.all_to_all(jnp.stack([panel_cols[:PANEL // row_count]] * lax.axis_siz...]
where the time goes in v1:
time: 771 us; the launch traced here: 762 us
  waiting for transfers between devices  369 us (48%)
  other arithmetic  165 us (21%)
  local copies, waits for them, and re-layouts  137 us (18%)
  matrix products  46.7 us (6%)
  starting transfers between devices  26.8 us (3%)
  between operations  17.8 us (2%)
    all_to_all x1, waiting for transfers between devices, on_device(): lax.all_to_all(onward, 'col', split_axis=1, concat_axis=1, tiled=True)  141 us
    all_gather x1, waiting for transfers between devices, on_device(): gathered = lax.all_gather(part, 'col', axis=0, tiled=False)  84.6 us
    another operation x15, other arithmetic, on_device(): lower_factor = jnp.linalg.cholesky(corner)  79.3 us
    ppermute x1, waiting for transfers between devices, on_device(): across = lax.ppermute(chosen, ('row', 'col'), pairs)  76.4 us
    all_to_all x1, waiting for transfers between devices, on_device(): lax.all_to_all(outgoing, 'row', split_axis=1, concat_axis=1, tiled=True)  46.6 us
    another operation x3, other arithmetic, on_device(): jax.scipy.linalg.solve_triangular(lower_factor, panel_cols.T, lower=True)  40.4 us
    gather x8, local copies, waits for them, and re-layouts, take_slabs(): return jnp.take(source, indices, axis=0)  32.2 us
    dot_general x1, matrix products, on_device(): update = jnp.einsum('rp,cp->rc', panel_factor, across, precision=exact_mode)  31.7 us
  transfers between devices with their start and end apart: 6, of which 6 were waited for; matrix products, arithmetic and copies ran while one was open for 2% of the time, Pallas kernels for 0%

profile of v1, /device:TPU:7, one launch (start us, length us, event | category | flops | bytes accessed | tf_op | source)
XLA Modules:
  0.0 762.4 jit_solution(14622390053163177061)
XLA Ops:
  29.0 46.6 %all-to-all-done = f32[2,1024,512]{2,0,1:T(2,128)} async-done(((f32[2,1024,512]{2,0,1:T(2,128)}), f32[2,1024,512]{2,0,1:T(2,128)}, u32[]{:S(2)}, u32[]{:S(2)}) %all-to-all-start) | async-done | bytes 4194336 | tf_op jit(solution)/shard_map/all_to_all | solution.py:66
  75.6 7.2 copy.128
  82.8 6.7 gather_fusion.4
  93.4 12.9 %copy.129 = f32[2,1024,1024]{2,0,1:T(2,128)} copy(f32[2,1024,1024]{2,1,0:T(8,128)S(1)} %fusion.2) | data formatting | bytes 16777216 | tf_op jit(solution)/shard_map/mul | solution.py:68
  106.3 8.1 %all-to-all-start.1 = ((f32[2,1024,1024]{2,0,1:T(2,128)}), f32[2,1024,1024]{2,0,1:T(2,128)}, u32[]{:S(2)}, u32[]{:S(2)}) async-start(f32[2,1024,1024]{2,0,1:T(2,128)} %copy.129), calls=%async_computation.1 | async-start | bytes 16777216 | tf_op jit(solution)/shard_map/all_to_all | solution.py:70
  115.9 140.9 %all-to-all-done.1 = f32[2,1024,1024]{2,0,1:T(2,128)} async-done(((f32[2,1024,1024]{2,0,1:T(2,128)}), f32[2,1024,1024]{2,0,1:T(2,128)}, u32[]{:S(2)}, u32[]{:S(2)}) %all-to-all-start.1) | async-done | bytes 8388640 | tf_op jit(solution)/shard_map/all_to_all | solution.py:70
  256.8 9.5 %copy.130 = f32[2,1024,1024]{2,1,0:T(8,128)} copy(f32[2,1024,1024]{2,0,1:T(2,128)} %all-to-all-done.1) | data formatting | bytes 16777216 | tf_op jit(solution)/shard_map/all_to_all | solution.py:70
  266.3 7.7 %gather_fusion.5 = f32[32,64,1024]{2,1,0:T(8,128)} fusion(f32[2,16,64,1024]{3,2,1,0:T(8,128)} %bitcast.131, s32[32]{0:T(128)S(1)} %reshape.541), kind=kCustom, calls=%fused_computation.5 | custom fusion | bytes 16777472 | tf_op jit(solution)/shard_map/vmap(jit(_take))/gather | solution.py:13
  274.0 6.0 fusion.1
  280.0 8.7 %copy.131 = f32[2,1024,1024]{2,1,0:T(8,128)} copy(f32[2,1024,1024]{1,2,0:T(8,128)} %fusion.1) | data formatting | bytes 16777216 | tf_op jit(solution)/shard_map/transpose | solution.py:84
  288.7 12.5 %gather_fusion.6 = f32[64,64,1024]{2,1,0:T(8,128)} fusion(f32[2,16,64,1024]{3,2,1,0:T(8,128)} %bitcast.126, s32[64]{0:T(128)S(1)} %reshape.547), kind=kCustom, calls=%fused_computation.6 | custom fusion | bytes 33554944 | tf_op jit(solution)/shard_map/vmap(jit(_take))/gather | solution.py:13
  301.2 7.3 select_multiply_fusion
  308.5 6.7 fusion.77
  315.2 9.7 %bitcast_add_fusion = f32[2048,1024]{1,0:T(8,128)S(1)} fusion(f32[1,32,64,1024]{3,2,1,0:T(8,128)} %get-tuple-element.35, f32[2048,1024]{1,0:T(8,128)} %param.4, f32[1,32,64,1024]{3,2,1,0:T(8,128)} %get-tuple-element.34), kind=kLoop, calls=%fused_computation.10 | loop fusion | flops 4194304 | bytes 33554432 | tf_op jit(solution)/shard_map/add | solution.py:87
  330.2 8.5 %collective-permute-done = f32[2048,64]{0,1:T(8,128)S(1)} collective-permute-done((f32[2048,64]{0,1:T(8,128)S(1)}, f32[2048,64]{0,1:T(8,128)S(1)}, u32[]{:S(2)}, u32[]{:S(2)}) %collective-permute-start) | collective-permute-done | bytes 524320 | tf_op jit(solution)/shard_map/ppermute | solution.py:91
  339.8 84.6 %all-gather.3.cloned.1.call-done = f32[16384,64]{1,0:T(8,128)} async-done(((f32[1024,64]{1,0:T(8,128)}), f32[16384,64]{1,0:T(8,128)}) %all-gather.3.cloned.1.call-update) | async-done | bytes 4194320 | tf_op jit(solution)/shard_map/all_gather | solution.py:99
  424.4 8.6 %copy.134 = f32[2,8,1024,64]{2,0,3,1:T(2,128)} copy(f32[2,8,1024,64]{3,2,1,0:T(8,128)} %bitcast.144) | data formatting | bytes 8388608 | tf_op jit(solution)/shard_map/reshape | solution.py:100
  440.5 5.7 all-to-all-start.2
  446.6 12.4 %all-to-all-done.2 = f32[8,64,512]{2,1,0:T(8,128)S(1)} async-done(((f32[8,64,512]{2,1,0:T(8,128)}), f32[8,64,512]{2,1,0:T(8,128)S(1)}, u32[]{:S(2)}, u32[]{:S(2)}) %all-to-all-start.2) | async-done | bytes 1048608 | tf_op jit(solution)/shard_map/all_to_all | solution.py:103
  459.6 11.7 %cholesky.104 = f32[128,128]{1,0:T(8,128)S(1)} custom-call(f32[128,128]{1,0:T(8,128)S(1)} %cholesky.266), custom_call_target="Cholesky" | custom-call | tf_op jit(solution)/shard_map/jit(cholesky)/cholesky | solution.py:108
  471.5 9.8 %custom-call.31 = f32[1,128,128]{1,2,0:T(8,128)S(1)} custom-call(f32[1,128,128]{2,1,0:T(8,128)S(1)} %get-tuple-element.45), custom_call_target="InvertDiagBlocksLowerTriangular" | custom-call | tf_op jit(solution)/shard_map/jit(cholesky)/cholesky | solution.py:108
  482.0 11.7 %cholesky.217 = f32[128,128]{1,0:T(8,128)S(1)} custom-call(f32[128,128]{1,0:T(8,128)S(1)} %cholesky.270), custom_call_target="Cholesky" | custom-call | tf_op jit(solution)/shard_map/jit(cholesky)/cholesky | solution.py:108
  495.1 9.9 %custom-call.32 = f32[1,128,128]{1,2,0:T(8,128)S(1)} custom-call(f32[1,128,128]{2,1,0:T(8,128)S(1)} %get-tuple-element.42), custom_call_target="InvertDiagBlocksLowerTriangular" | custom-call | tf_op jit(solution)/shard_map/jit(cholesky)/cholesky | solution.py:108
  505.7 11.7 %cholesky.238 = f32[128,128]{1,0:T(8,128)S(1)} custom-call(f32[128,128]{1,0:T(8,128)S(1)} %cholesky.275), custom_call_target="Cholesky" | custom-call | tf_op jit(solution)/shard_map/jit(cholesky)/cholesky | solution.py:108
  518.1 9.8 %custom-call.33 = f32[1,128,128]{1,2,0:T(8,128)S(1)} custom-call(f32[1,128,128]{2,1,0:T(8,128)S(1)} %get-tuple-element.39), custom_call_target="InvertDiagBlocksLowerTriangular" | custom-call | tf_op jit(solution)/shard_map/jit(cholesky)/cholesky | solution.py:108
  528.5 11.7 %cholesky.255 = f32[128,128]{1,0:T(8,128)S(1)} custom-call(f32[128,128]{1,0:T(8,128)S(1)} %convolution_subtract_fusion.4), custom_call_target="Cholesky" | custom-call | tf_op jit(solution)/shard_map/jit(cholesky)/cholesky | solution.py:108
  544.0 10.5 %while.1 = (s32[]{:T(128)}, f32[512,512]{1,0:T(8,128)S(1)}, s32[4,2]{0,1:T(2,128)S(1)}, f32[4,128,128]{2,1,0:T(8,128)}, s32[]{:T(128)}) while((s32[]{:T(128)}, f32[512,512]{1,0:T(8,128)S(1)}, s32[4,2]{0,1:T(2,128)S(1)}, f32[4,128,128]{2,1,0:T(8,128)}, s32[]{:T(128)}) %tuple.44), condition=%wide.while_cond, body=%wide.while_body.sunk | while | flops 2 | bytes 132705 | solution.py:109
  554.5 40.2 %custom-call.34 = f32[4,128,128]{1,2,0:T(8,128)S(1)} custom-call(f32[4,128,128]{2,1,0:T(8,128)} %get-tuple-element.9), custom_call_target="InvertDiagBlocksLowerTriangular" | custom-call | tf_op jit(solution)/shard_map/jit(_solve_triangular)/triangular_solve | solution.py:109
  611.4 5.6 copy.140
  624.0 6.4 collective-permute-start.1
  647.0 76.4 %collective-permute-done.1 = f32[1024,512]{1,0:T(8,128)} collective-permute-done((f32[1024,512]{1,0:T(8,128)}, f32[1024,512]{1,0:T(8,128)}, u32[]{:S(2)}, u32[]{:S(2)}) %collective-permute-start.1) | collective-permute-done | bytes 2097184 | tf_op jit(solution)/shard_map/ppermute | solution.py:127
  723.4 31.7 %subtract_select_fusion = f32[2048,1024]{1,0:T(8,128)} fusion(f32[2048,1024]{1,0:T(8,128)} %copy-done, pred[1024]{0:T(1024)(128)(4,1)S(1)} %fusion.54, pred[2048]{0:T(1024)(128)(4,1)S(1)} %fusion.48, f32[2048,512]{0,1:T(8,128)} %select_select_fusion, f32[1024,512]{1,0:T(8,128)} %collective-permute-done.1), kind=kOutput, calls=%fused_computation.17 | convolution fusion | flops 12891193344 | bytes 23071744 | tf_op jit(solution)/shard_map/rp,cp->rc/dot_general | solution.py:128
  (153 shorter events, 97.6 us)
Async XLA Ops:
  23.4 52.2 %all-to-all-start = ((f32[2,1024,512]{2,0,1:T(2,128)}), f32[2,1024,512]{2,0,1:T(2,128)}, u32[]{:S(2)}, u32[]{:S(2)}) async-start(f32[2,1024,512]{2,0,1:T(2,128)} %copy.127), calls=%async_computation | async-start | bytes 8388608 | tf_op jit(solution)/shard_map/all_to_all | solution.py:66
  106.3 8.4 %copy-start.7 = (s32[2,128]{1,0:T(2,128)S(1)}, s32[2,128]{1,0:T(2,128)}, u32[]{:S(2)}) copy-start(s32[2,128]{1,0:T(2,128)} %param.6) | copy-start | bytes 3076
  106.3 8.8 %copy-start.8 = (s32[2,128]{1,0:T(2,128)S(1)}, s32[2,128]{1,0:T(2,128)}, u32[]{:S(2)}) copy-start(s32[2,128]{1,0:T(2,128)} %param.7) | copy-start | bytes 3076
  106.3 150.5 %all-to-all-start.1 = ((f32[2,1024,1024]{2,0,1:T(2,128)}), f32[2,1024,1024]{2,0,1:T(2,128)}, u32[]{:S(2)}, u32[]{:S(2)}) async-start(f32[2,1024,1024]{2,0,1:T(2,128)} %copy.129), calls=%async_computation.1 | async-start | bytes 16777216 | tf_op jit(solution)/shard_map/all_to_all | solution.py:70
  114.4 310.0 %all-gather.3.cloned.1.call-start = ((), (), s32[]{:S(2)}) async-start(), calls=%async_computation.3 | async-start | bytes 8912896 | tf_op jit(solution)/shard_map/all_gather | solution.py:99
  325.0 3.4 copy-start
  328.8 9.9 %collective-permute-start = (f32[2048,64]{0,1:T(8,128)S(1)}, f32[2048,64]{0,1:T(8,128)S(1)}, u32[]{:S(2)}, u32[]{:S(2)}) collective-permute-start(f32[2048,64]{0,1:T(8,128)S(1)} %copy.132), channel_id=1, source_target_pairs={{0,8},{1,9},{2,10},{3,11},{4,12},{5,13},{6,14},{7,15},{16,24},{17,... | collective-permute-start | bytes 1572872 | tf_op jit(solution)/shard_map/ppermute | solution.py:91
  437.2 2.0 copy-start.1
  440.5 18.5 %all-to-all-start.2 = ((f32[8,64,512]{2,1,0:T(8,128)}), f32[8,64,512]{2,1,0:T(8,128)S(1)}, u32[]{:S(2)}, u32[]{:S(2)}) async-start(f32[8,64,512]{2,1,0:T(8,128)} %stack.2), calls=%async_computation.2 | async-start | bytes 2097152 | tf_op jit(solution)/shard_map/all_to_all | solution.py:103
  554.5 42.6 %copy-start.6 = (f32[512,512]{1,0:T(8,128)}, f32[512,512]{1,0:T(8,128)S(1)}, u32[]{:S(2)}) copy-start(f32[512,512]{1,0:T(8,128)S(1)} %get-tuple-element.111) | copy-start | bytes 3145732
  594.7 5.7 copy-start.2
  603.7 4.2 copy-start.3
  607.9 1.1 copy-start.5
  624.0 99.3 %collective-permute-start.1 = (f32[1024,512]{1,0:T(8,128)}, f32[1024,512]{1,0:T(8,128)}, u32[]{:S(2)}, u32[]{:S(2)}) collective-permute-start(f32[1024,512]{1,0:T(8,128)} %bitcast.41), channel_id=1, source_target_pairs={{0,0},{1,16},{2,32},{3,48},{4,64},{5,80},{6,96},{7,112},{8,8},{9,2... | collective-permute-start | bytes 6291464 | tf_op jit(solution)/shard_map/ppermute | solution.py:127
  630.8 5.5 copy-start.4
Sparse Core Ops, SparseCore 0:
  339.9 84.4 all-gather.2
